TPU v7x, 32 devices: a whole 2x2x4 slice. The times are simulated.
32 devices in a mesh: grp: 2 (over y), tile: 4 (over z), freq: 4 (over x, core).
Axes of the slice: x: 2, y: 2, z: 4, core: 2. Of those that a mesh axis runs over, the one named last changes fastest.
Arguments:
- sources: bfloat16 [4, 4, 2048, 512], P('freq', 'grp', 'tile'), parts along dimension 1, may hold values from -6 to 6
- v_factors: bfloat16 [4, 4, 2, 4, 112, 512], P('freq', 'tile', None, 'grp'), parts along dimension 3, may hold values from -0.1875 to 0.1875
- u_factors: bfloat16 [4, 4, 4, 112, 1024], P('freq', None, 'grp', None, 'tile'), parts along dimension 2, may hold values from -0.1875 to 0.1875
- tile_ranks: int32 [4, 4, 4], P('freq', 'grp', 'tile'), parts along dimension 1, may hold values from 16 to 112, as said below
- window_bounds: int32 [4, 1024, 512], P('grp', ('tile', 'freq')), parts along dimension 0, may hold values from 0 to 31, as said below
Outputs:
- windowed_traces: float32 [1024, 64, 512], P(('tile', 'freq'), 'grp'), parts along dimension 1
There are 2 independent parts, one for each index of `grp`. A program takes and returns all parts, laid end to end along the dimension named above; each array names one. Nothing has to cross between parts.
Inputs may be any that keep to these rules, and one draw needn't show every extreme that they name: `tile_ranks`: each tile's rank for each frequency; rank slots at or beyond it carry no coefficients. window_bounds[1] - window_bounds[0] lies between 8 and 16 for every receiver and virtual source.
All inputs are finite; a program needn't handle non-finite values.
Results may differ from a plain program's by a relative error of at most 0.0041.
Values may be sent and summed in bfloat16 or wider, within the bound.
No kernel may reach another device: no remote copies, remote signals or barrier semaphores. Data moves between devices by JAX's collectives and lax.ppermute only.
A program may use at most 64 MiB of HBM per device.

v0:
```python
import math
import jax
import jax.numpy as jnp
from jax import lax
from jax.sharding import PartitionSpec as P

NT = 32
S_CHUNKS = 2
first_bin = 2


def inverse_tables(count_freq, count_time):
    freq_index = jnp.arange(count_freq, dtype=jnp.int32)[:, None] + first_bin
    time_index = jnp.arange(count_time, dtype=jnp.int32)[None, :]
    phase_step = freq_index * time_index % count_time
    angles = phase_step.astype(jnp.float32) * (2.0 * math.pi / count_time)
    return (jnp.cos(angles), jnp.sin(angles))


def column_products(v_local, x_local, rank_local):
    products = lax.dot_general(
        v_local, x_local, (((3,), (1,)), ((), ())), preferred_element_type=jnp.float32
    )
    coef_real = products[:, 0, :, 0] - products[:, 1, :, 1]
    coef_imag = products[:, 0, :, 1] + products[:, 1, :, 0]
    slot_index = jnp.arange(v_local.shape[2], dtype=jnp.int32)
    live_slots = slot_index[None, :, None] < rank_local[:, None, None]
    coef_real = jnp.where(live_slots, coef_real, jnp.float32(0.0)).astype(jnp.bfloat16)
    coef_imag = jnp.where(live_slots, coef_imag, jnp.float32(0.0)).astype(jnp.bfloat16)
    return jnp.stack([coef_real, coef_imag], axis=1)


def row_spectrum(u_local, blocks):
    products = lax.dot_general(
        u_local, blocks, (((0, 2), (0, 2)), ((), ())), preferred_element_type=jnp.float32
    )
    real_part = products[0, :, 0] - products[1, :, 1]
    imag_part = products[0, :, 1] + products[1, :, 0]
    return jnp.stack([real_part, imag_part], axis=0).astype(jnp.bfloat16)


def relay_exchange(own, u_local):
    t = lax.axis_index("tile")
    up = [(0, 1), (1, 2), (2, 3)]
    down = [(1, 0), (2, 1), (3, 2)]
    up1 = lax.ppermute(own[1], "tile", up)
    down1 = lax.ppermute(own[0], "tile", down)
    up2 = lax.ppermute(jnp.where(t == 0, own[0], up1), "tile", up)
    down2 = lax.ppermute(jnp.where(t == 3, own[1], down1), "tile", down)
    up3 = lax.ppermute(up2, "tile", [(2, 3)])
    down3 = lax.ppermute(down2, "tile", [(1, 0)])
    orders = (
        lambda: (own[0], down1, down2, down3),
        lambda: (up2, own[0], down1, down2),
        lambda: (up2, up1, own[1], down2),
        lambda: (up3, up2, up1, own[1]),
    )
    branches = [
        (lambda order: lambda: row_spectrum(u_local, jnp.stack(order(), axis=0)))(order)
        for order in orders
    ]
    return lax.switch(t, branches)


def gather_exchange(own, u_local, n_tile):
    repeat = n_tile // own.shape[0]
    sending = jnp.repeat(own, repeat, axis=0)
    received = lax.all_to_all(sending, "tile", split_axis=0, concat_axis=0, tiled=True)
    return row_spectrum(u_local, received)


def make_per_device(n_tile):

    def per_device(sources, v_factors, u_factors, tile_ranks, window_bounds):
        v_local = v_factors[0, 0]
        u_local = u_factors[0]
        x_local = sources[0]
        rank_local = tile_ranks[0, :, 0]
        rows = v_local.shape[0]
        use_relay = n_tile == 4 and rows == 2 and (u_local.shape[0] == 4)
        count_s = x_local.shape[2]
        chunks = S_CHUNKS if count_s % S_CHUNKS == 0 else 1
        width = count_s // chunks
        received_parts = []
        for c in range(chunks):
            x_part = x_local[:, :, c * width : (c + 1) * width]
            own = column_products(v_local, x_part, rank_local)
            if use_relay:
                spectrum = relay_exchange(own, u_local)
            else:
                spectrum = gather_exchange(own, u_local, n_tile)
            received_parts.append(
                lax.all_to_all(spectrum[None], "freq", split_axis=2, concat_axis=0, tiled=True)
            )
        received = jnp.concatenate(received_parts, axis=3) if chunks > 1 else received_parts[0]
        count_freq = received.shape[0]
        cosine_table, sine_table = inverse_tables(count_freq, NT)
        widened = received.astype(jnp.float32)
        real_sum = 0.0
        imag_sum = 0.0
        for f in range(count_freq):
            real_sum = real_sum + widened[f, 0][:, None, :] * cosine_table[f][None, :, None]
            imag_sum = imag_sum + widened[f, 1][:, None, :] * sine_table[f][None, :, None]
        traces = (real_sum - imag_sum) * (1.0 / math.sqrt(count_freq))
        time_index = jnp.arange(NT, dtype=jnp.int32)[None, :, None]
        inside = (time_index >= window_bounds[0][:, None, :]) & (
            time_index < window_bounds[1][:, None, :]
        )
        return jnp.where(inside, traces, jnp.float32(0.0))

    return per_device


def solution(mesh):
    return jax.shard_map(
        make_per_device(mesh.shape["tile"]),
        mesh=mesh,
        in_specs=(
            P("freq", "grp", "tile", None),
            P("freq", "tile", None, "grp", None, None),
            P("freq", None, "grp", None, "tile"),
            P("freq", "grp", "tile"),
            P("grp", ("tile", "freq"), None),
        ),
        out_specs=P(("tile", "freq"), "grp", None),
        check_vma=False,
    )
```

profile of v0, /device:TPU:0, one launch (start us, length us, event | category | flops | bytes accessed | tf_op | source)
XLA Modules:
  0.0 69.7 jit_solution(6855587100608741447)
XLA Ops:
  0.0 0.0 copy-start
  0.0 0.0 copy-start.2
  0.0 1.0 %copy-done = bf16[1,1,2,2,112,512]{5,4,3,2,1,0:T(8,128)(2,1)S(1)} copy-done((bf16[1,1,2,2,112,512]{5,4,3,2,1,0:T(8,128)(2,1)S(1)}, bf16[1,1,2,2,112,512]{5,4,3,2,1,0:T(8,128)(2,1)}, u32[]{:S(2)}) %copy-start) | copy-done | bytes 458776
  1.0 1.5 %fusion.90 = f32[2,2,112,2,256]{4,2,3,1,0:T(8,128)S(1)} fusion(bf16[2,512,512]{2,1,0:T(8,128)(2,1)} %bitcast.377, bf16[1,1,2,2,112,512]{5,4,3,2,1,0:T(8,128)(2,1)S(1)} %copy-done), kind=kOutput, calls=%fused_computation.143 | convolution fusion | flops 234881024 | bytes 1900544 | tf_op jit(solution)/shard_map/dot_general | solution.py:21
  2.5 1.4 %fusion.89 = f32[2,2,112,2,256]{4,2,0,3,1:T(8,128)S(1)} fusion(bf16[2,512,512]{2,1,0:T(8,128)(2,1)} %bitcast.378, bf16[1,1,2,2,112,512]{5,4,3,2,1,0:T(8,128)(2,1)S(1)} %copy-done), kind=kOutput, calls=%fused_computation.141 | convolution fusion | flops 234881024 | bytes 1900544 | tf_op jit(solution)/shard_map/dot_general | solution.py:21
  4.0 0.7 %iota_compare_fusion.2 = pred[2,112]{1,0:T(4,128)(4,1)S(1)} fusion(s32[2]{0:T(128)} %bitcast.408), kind=kLoop, calls=%fused_computation.207 | loop fusion | flops 224 | bytes 232 | tf_op jit(solution)/shard_map/lt | solution.py:27
  4.7 0.1 fusion.101
  4.8 0.1 fusion.98
  5.0 4.9 %collective-permute-start.3 = (bf16[2,112,256]{2,1,0:T(8,128)(2,1)S(1)}, bf16[2,112,256]{2,1,0:T(8,128)(2,1)S(1)}, u32[]{:S(2)}, u32[]{:S(2)}) collective-permute-start(bf16[2,112,256]{2,1,0:T(8,128)(2,1)S(1)} %fusion.114), channel_id=1, source_target_pairs={{0,4},{4,8},{8,12},{1,5},{5,9},{9,13},{2,6},{6,10},{10,14},{3,7},{... | collective-permute-start | bytes 344072 | tf_op jit(solution)/shard_map/ppermute | solution.py:46
  9.9 3.5 %collective-permute-start.9 = (bf16[2,112,256]{2,1,0:T(8,128)(2,1)S(1)}, bf16[2,112,256]{2,1,0:T(8,128)(2,1)S(1)}, u32[]{:S(2)}, u32[]{:S(2)}) collective-permute-start(bf16[2,112,256]{2,1,0:T(8,128)(2,1)S(1)} %fusion.110), channel_id=1, source_target_pairs={{0,4},{4,8},{8,12},{1,5},{5,9},{9,13},{2,6},{6,10},{10,14},{3,7},{... | collective-permute-start | bytes 344072 | tf_op jit(solution)/shard_map/ppermute | solution.py:46
  13.4 0.0 copy-done.2
  13.5 2.3 %collective-permute-done.9 = bf16[2,112,256]{2,1,0:T(8,128)(2,1)S(1)} collective-permute-done((bf16[2,112,256]{2,1,0:T(8,128)(2,1)S(1)}, bf16[2,112,256]{2,1,0:T(8,128)(2,1)S(1)}, u32[]{:S(2)}, u32[]{:S(2)}) %collective-permute-start.9) | collective-permute-done | bytes 114720 | tf_op jit(solution)/shard_map/ppermute | solution.py:46
  15.8 5.0 %collective-permute-start.10 = (bf16[2,112,256]{2,1,0:T(8,128)(2,1)S(1)}, bf16[2,112,256]{2,1,0:T(8,128)(2,1)}, u32[]{:S(2)}, u32[]{:S(2)}) collective-permute-start(bf16[2,112,256]{2,1,0:T(8,128)(2,1)S(1)} %get-tuple-element.201), channel_id=1, source_target_pairs={{0,4},{4,8},{8,12},{1,5},{5,9},{9,13},{2,6},{6,10},{10,14},{3,7},{... | collective-permute-start | bytes 344072 | tf_op jit(solution)/shard_map/ppermute | solution.py:48
  20.8 1.3 %collective-permute-start.6 = (bf16[2,112,256]{2,1,0:T(8,128)(2,1)S(1)}, bf16[2,112,256]{2,1,0:T(8,128)(2,1)S(1)}, u32[]{:S(2)}, u32[]{:S(2)}) collective-permute-start(bf16[2,112,256]{2,1,0:T(8,128)(2,1)S(1)} %get-tuple-element.202), channel_id=1, source_target_pairs={{4,0},{8,4},{12,8},{5,1},{9,5},{13,9},{6,2},{10,6},{14,10},{7,3},{... | collective-permute-start | bytes 344072 | tf_op jit(solution)/shard_map/ppermute | solution.py:47
  22.1 0.0 collective-permute-done.3
  22.1 1.3 %collective-permute-start = (bf16[2,112,256]{2,1,0:T(8,128)(2,1)S(1)}, bf16[2,112,256]{2,1,0:T(8,128)(2,1)S(1)}, u32[]{:S(2)}, u32[]{:S(2)}) collective-permute-start(bf16[2,112,256]{2,1,0:T(8,128)(2,1)S(1)} %get-tuple-element.200), channel_id=1, source_target_pairs={{4,0},{8,4},{12,8},{5,1},{9,5},{13,9},{6,2},{10,6},{14,10},{7,3},{... | collective-permute-start | bytes 344072 | tf_op jit(solution)/shard_map/ppermute | solution.py:47
  23.4 4.4 %collective-permute-done.6 = bf16[2,112,256]{2,1,0:T(8,128)(2,1)S(1)} collective-permute-done((bf16[2,112,256]{2,1,0:T(8,128)(2,1)S(1)}, bf16[2,112,256]{2,1,0:T(8,128)(2,1)S(1)}, u32[]{:S(2)}, u32[]{:S(2)}) %collective-permute-start.6) | collective-permute-done | bytes 114720 | tf_op jit(solution)/shard_map/ppermute | solution.py:47
  27.8 1.3 %collective-permute-start.7 = (bf16[2,112,256]{2,1,0:T(8,128)(2,1)S(1)}, bf16[2,112,256]{2,1,0:T(8,128)(2,1)S(1)}, u32[]{:S(2)}, u32[]{:S(2)}) collective-permute-start(bf16[2,112,256]{2,1,0:T(8,128)(2,1)S(1)} %broadcast_select_fusion.2), channel_id=1, source_target_pairs={{4,0},{8,4},{12,8},{5,1},{9,5},{13,9},{6,2},{10,6},{14,10},{7,3},{... | collective-permute-start | bytes 344072 | tf_op jit(solution)/shard_map/ppermute | solution.py:49
  29.1 0.0 copy-done.1
  29.2 4.6 %collective-permute-start.4 = (bf16[2,112,256]{2,1,0:T(8,128)(2,1)S(1)}, bf16[2,112,256]{2,1,0:T(8,128)(2,1)S(1)}, u32[]{:S(2)}, u32[]{:S(2)}) collective-permute-start(bf16[2,112,256]{2,1,0:T(8,128)(2,1)S(1)} %get-tuple-element.199), channel_id=1, source_target_pairs={{0,4},{4,8},{8,12},{1,5},{5,9},{9,13},{2,6},{6,10},{10,14},{3,7},{... | collective-permute-start | bytes 344072 | tf_op jit(solution)/shard_map/ppermute | solution.py:48
  33.8 0.0 collective-permute-done.10
  33.8 0.7 collective-permute-start.11
  34.5 0.0 collective-permute-done.7
  34.5 1.3 %collective-permute-start.8 = (bf16[2,112,256]{2,1,0:T(8,128)(2,1)S(1)}, bf16[2,112,256]{2,1,0:T(8,128)(2,1)S(1)}, u32[]{:S(2)}, u32[]{:S(2)}) collective-permute-start(bf16[2,112,256]{2,1,0:T(8,128)(2,1)S(1)} %collective-permute-done.7), channel_id=1, source_target_pairs={{4,0},{5,1},{6,2},{7,3},{20,16},{21,17},{22,18},{23,19}} | collective-permute-start | bytes 344072 | tf_op jit(solution)/shard_map/ppermute | solution.py:51
  35.8 0.0 collective-permute-done
  35.8 1.3 %collective-permute-start.1 = (bf16[2,112,256]{2,1,0:T(8,128)(2,1)S(1)}, bf16[2,112,256]{2,1,0:T(8,128)(2,1)S(1)}, u32[]{:S(2)}, u32[]{:S(2)}) collective-permute-start(bf16[2,112,256]{2,1,0:T(8,128)(2,1)S(1)} %broadcast_select_fusion.3), channel_id=1, source_target_pairs={{4,0},{8,4},{12,8},{5,1},{9,5},{13,9},{6,2},{10,6},{14,10},{7,3},{... | collective-permute-start | bytes 344072 | tf_op jit(solution)/shard_map/ppermute | solution.py:49
  37.1 0.0 collective-permute-done.11
  37.1 4.0 %collective-permute-done.8 = bf16[2,112,256]{2,1,0:T(8,128)(2,1)S(1)} collective-permute-done((bf16[2,112,256]{2,1,0:T(8,128)(2,1)S(1)}, bf16[2,112,256]{2,1,0:T(8,128)(2,1)S(1)}, u32[]{:S(2)}, u32[]{:S(2)}) %collective-permute-start.8) | collective-permute-done | bytes 114720 | tf_op jit(solution)/shard_map/ppermute | solution.py:51
  41.2 0.6 conditional.5
  41.2 0.5 convolution_bitcast_fusion.4
  41.8 0.9 %copy.148 = bf16[2,256,256]{2,0,1:T(2,128)(2,1)} copy(bf16[2,256,256]{1,2,0:T(8,128)(2,1)S(1)} %get-tuple-element.231) | data formatting | bytes 524288
  42.7 3.4 %all-to-all-start.1 = ((bf16[1,2,256,256]{3,1,0,2:T(2,128)(2,1)}), bf16[1,2,256,256]{3,1,0,2:T(2,128)(2,1)S(1)}, u32[]{:S(2)}, u32[]{:S(2)}) async-start(bf16[1,2,256,256]{3,1,0,2:T(2,128)(2,1)} %bitcast.124), calls=%async_computation.1 | async-start | bytes 524288 | tf_op jit(solution)/shard_map/all_to_all | solution.py:93
  46.1 0.1 fusion.119
  46.2 0.0 collective-permute-done.4
  46.2 0.7 collective-permute-start.5
  46.9 0.0 collective-permute-done.1
  46.9 1.3 %collective-permute-start.2 = (bf16[2,112,256]{2,1,0:T(8,128)(2,1)S(1)}, bf16[2,112,256]{2,1,0:T(8,128)(2,1)S(1)}, u32[]{:S(2)}, u32[]{:S(2)}) collective-permute-start(bf16[2,112,256]{2,1,0:T(8,128)(2,1)S(1)} %collective-permute-done.1), channel_id=1, source_target_pairs={{4,0},{5,1},{6,2},{7,3},{20,16},{21,17},{22,18},{23,19}} | collective-permute-start | bytes 344072 | tf_op jit(solution)/shard_map/ppermute | solution.py:51
  48.2 0.0 collective-permute-done.5
  48.2 6.1 %collective-permute-done.2 = bf16[2,112,256]{2,1,0:T(8,128)(2,1)S(1)} collective-permute-done((bf16[2,112,256]{2,1,0:T(8,128)(2,1)S(1)}, bf16[2,112,256]{2,1,0:T(8,128)(2,1)S(1)}, u32[]{:S(2)}, u32[]{:S(2)}) %collective-permute-start.2) | collective-permute-done | bytes 114720 | tf_op jit(solution)/shard_map/ppermute | solution.py:51
  54.3 0.6 conditional.4
  54.3 0.5 convolution_bitcast_fusion
  54.9 0.9 %copy.147 = bf16[2,256,256]{2,0,1:T(2,128)(2,1)} copy(bf16[2,256,256]{1,2,0:T(8,128)(2,1)S(1)} %get-tuple-element.230) | data formatting | bytes 524288
  55.8 0.0 all-to-all-done.1
  55.8 3.4 %all-to-all-start = ((bf16[1,2,256,256]{3,1,0,2:T(2,128)(2,1)}), bf16[1,2,256,256]{3,1,0,2:T(2,128)(2,1)S(1)}, u32[]{:S(2)}, u32[]{:S(2)}) async-start(bf16[1,2,256,256]{3,1,0,2:T(2,128)(2,1)} %bitcast.113), calls=%async_computation | async-start | bytes 524288 | tf_op jit(solution)/shard_map/all_to_all | solution.py:93
  59.2 5.9 %all-to-all-done = bf16[1,2,256,256]{3,1,0,2:T(2,128)(2,1)S(1)} async-done(((bf16[1,2,256,256]{3,1,0,2:T(2,128)(2,1)}), bf16[1,2,256,256]{3,1,0,2:T(2,128)(2,1)S(1)}, u32[]{:S(2)}, u32[]{:S(2)}) %all-to-all-start) | async-done | bytes 262176 | tf_op jit(solution)/shard_map/all_to_all | solution.py:93
  65.2 0.1 maximum_convert_fusion
  65.3 0.1 slice_bitcast_fusion.29
  65.4 4.3 %multiply_select_fusion = f32[64,32,512]{2,1,0:T(8,128)} fusion(f32[32]{0:T(128)S(1)} %get-tuple-element.220, f32[64,512]{1,0:T(8,128)S(1)} %get-tuple-element.204, f32[32]{0:T(128)S(1)} %get-tuple-element.221, f32[64,512]{1,0:T(8,128)S(1)} %get-tuple-element.205, f32[32]{0:T(128)S(1)} %get-tuple-element.222, f32[64,512]{1,0:T(8,128)S(1)} %get-tuple-element.206, ...), kind=kLoop, calls=%fused_computation.136 | loop fusion | flops 20971520 | bytes 5506048 | tf_op jit(solution)/shard_map/jit(_where)/select_n | solution.py:109
  (24 shorter events, 0.5 us)
Async XLA Ops:
  0.0 1.0 %copy-start = (bf16[1,1,2,2,112,512]{5,4,3,2,1,0:T(8,128)(2,1)S(1)}, bf16[1,1,2,2,112,512]{5,4,3,2,1,0:T(8,128)(2,1)}, u32[]{:S(2)}) copy-start(bf16[1,1,2,2,112,512]{5,4,3,2,1,0:T(8,128)(2,1)} %param.14) | copy-start | bytes 1376260
  0.0 13.4 %copy-start.2 = (s32[2,64,512]{2,1,0:T(8,128)S(1)}, s32[2,64,512]{2,1,0:T(8,128)}, u32[]{:S(2)}) copy-start(s32[2,64,512]{2,1,0:T(8,128)} %param.17) | copy-start | bytes 786436
  1.0 28.1 %copy-start.1 = (bf16[1,4,2,112,256]{4,3,2,1,0:T(8,128)(2,1)S(1)}, bf16[1,4,2,112,256]{4,3,2,1,0:T(8,128)(2,1)}, u32[]{:S(2)}) copy-start(bf16[1,4,2,112,256]{4,3,2,1,0:T(8,128)(2,1)} %param.15) | copy-start | bytes 1376260
  5.0 17.1 %collective-permute-start.3 = (bf16[2,112,256]{2,1,0:T(8,128)(2,1)S(1)}, bf16[2,112,256]{2,1,0:T(8,128)(2,1)S(1)}, u32[]{:S(2)}, u32[]{:S(2)}) collective-permute-start(bf16[2,112,256]{2,1,0:T(8,128)(2,1)S(1)} %fusion.114), channel_id=1, source_target_pairs={{0,4},{4,8},{8,12},{1,5},{5,9},{9,13},{2,6},{6,10},{10,14},{3,7},{... | collective-permute-start | bytes 344072 | tf_op jit(solution)/shard_map/ppermute | solution.py:46
  9.9 5.8 %collective-permute-start.9 = (bf16[2,112,256]{2,1,0:T(8,128)(2,1)S(1)}, bf16[2,112,256]{2,1,0:T(8,128)(2,1)S(1)}, u32[]{:S(2)}, u32[]{:S(2)}) collective-permute-start(bf16[2,112,256]{2,1,0:T(8,128)(2,1)S(1)} %fusion.110), channel_id=1, source_target_pairs={{0,4},{4,8},{8,12},{1,5},{5,9},{9,13},{2,6},{6,10},{10,14},{3,7},{... | collective-permute-start | bytes 344072 | tf_op jit(solution)/shard_map/ppermute | solution.py:46
  15.8 18.0 %collective-permute-start.10 = (bf16[2,112,256]{2,1,0:T(8,128)(2,1)S(1)}, bf16[2,112,256]{2,1,0:T(8,128)(2,1)}, u32[]{:S(2)}, u32[]{:S(2)}) collective-permute-start(bf16[2,112,256]{2,1,0:T(8,128)(2,1)S(1)} %get-tuple-element.201), channel_id=1, source_target_pairs={{0,4},{4,8},{8,12},{1,5},{5,9},{9,13},{2,6},{6,10},{10,14},{3,7},{... | collective-permute-start | bytes 344072 | tf_op jit(solution)/shard_map/ppermute | solution.py:48
  20.8 7.0 %collective-permute-start.6 = (bf16[2,112,256]{2,1,0:T(8,128)(2,1)S(1)}, bf16[2,112,256]{2,1,0:T(8,128)(2,1)S(1)}, u32[]{:S(2)}, u32[]{:S(2)}) collective-permute-start(bf16[2,112,256]{2,1,0:T(8,128)(2,1)S(1)} %get-tuple-element.202), channel_id=1, source_target_pairs={{4,0},{8,4},{12,8},{5,1},{9,5},{13,9},{6,2},{10,6},{14,10},{7,3},{... | collective-permute-start | bytes 344072 | tf_op jit(solution)/shard_map/ppermute | solution.py:47
  22.1 13.7 %collective-permute-start = (bf16[2,112,256]{2,1,0:T(8,128)(2,1)S(1)}, bf16[2,112,256]{2,1,0:T(8,128)(2,1)S(1)}, u32[]{:S(2)}, u32[]{:S(2)}) collective-permute-start(bf16[2,112,256]{2,1,0:T(8,128)(2,1)S(1)} %get-tuple-element.200), channel_id=1, source_target_pairs={{4,0},{8,4},{12,8},{5,1},{9,5},{13,9},{6,2},{10,6},{14,10},{7,3},{... | collective-permute-start | bytes 344072 | tf_op jit(solution)/shard_map/ppermute | solution.py:47
  27.8 6.7 %collective-permute-start.7 = (bf16[2,112,256]{2,1,0:T(8,128)(2,1)S(1)}, bf16[2,112,256]{2,1,0:T(8,128)(2,1)S(1)}, u32[]{:S(2)}, u32[]{:S(2)}) collective-permute-start(bf16[2,112,256]{2,1,0:T(8,128)(2,1)S(1)} %broadcast_select_fusion.2), channel_id=1, source_target_pairs={{4,0},{8,4},{12,8},{5,1},{9,5},{13,9},{6,2},{10,6},{14,10},{7,3},{... | collective-permute-start | bytes 344072 | tf_op jit(solution)/shard_map/ppermute | solution.py:49
  29.2 17.0 %collective-permute-start.4 = (bf16[2,112,256]{2,1,0:T(8,128)(2,1)S(1)}, bf16[2,112,256]{2,1,0:T(8,128)(2,1)S(1)}, u32[]{:S(2)}, u32[]{:S(2)}) collective-permute-start(bf16[2,112,256]{2,1,0:T(8,128)(2,1)S(1)} %get-tuple-element.199), channel_id=1, source_target_pairs={{0,4},{4,8},{8,12},{1,5},{5,9},{9,13},{2,6},{6,10},{10,14},{3,7},{... | collective-permute-start | bytes 344072 | tf_op jit(solution)/shard_map/ppermute | solution.py:48
  33.8 3.3 %collective-permute-start.11 = (bf16[2,112,256]{2,1,0:T(8,128)(2,1)}, bf16[2,112,256]{2,1,0:T(8,128)(2,1)S(1)}, u32[]{:S(2)}, u32[]{:S(2)}) collective-permute-start(bf16[2,112,256]{2,1,0:T(8,128)(2,1)} %collective-permute-done.10), channel_id=1, source_target_pairs={{8,12},{9,13},{10,14},{11,15},{24,28},{25,29},{26,30},{27,31}} | collective-permute-start | bytes 344072 | tf_op jit(solution)/shard_map/ppermute | solution.py:50
  34.5 6.7 %collective-permute-start.8 = (bf16[2,112,256]{2,1,0:T(8,128)(2,1)S(1)}, bf16[2,112,256]{2,1,0:T(8,128)(2,1)S(1)}, u32[]{:S(2)}, u32[]{:S(2)}) collective-permute-start(bf16[2,112,256]{2,1,0:T(8,128)(2,1)S(1)} %collective-permute-done.7), channel_id=1, source_target_pairs={{4,0},{5,1},{6,2},{7,3},{20,16},{21,17},{22,18},{23,19}} | collective-permute-start | bytes 344072 | tf_op jit(solution)/shard_map/ppermute | solution.py:51
  35.8 11.1 %collective-permute-start.1 = (bf16[2,112,256]{2,1,0:T(8,128)(2,1)S(1)}, bf16[2,112,256]{2,1,0:T(8,128)(2,1)S(1)}, u32[]{:S(2)}, u32[]{:S(2)}) collective-permute-start(bf16[2,112,256]{2,1,0:T(8,128)(2,1)S(1)} %broadcast_select_fusion.3), channel_id=1, source_target_pairs={{4,0},{8,4},{12,8},{5,1},{9,5},{13,9},{6,2},{10,6},{14,10},{7,3},{... | collective-permute-start | bytes 344072 | tf_op jit(solution)/shard_map/ppermute | solution.py:49
  42.7 13.1 %all-to-all-start.1 = ((bf16[1,2,256,256]{3,1,0,2:T(2,128)(2,1)}), bf16[1,2,256,256]{3,1,0,2:T(2,128)(2,1)S(1)}, u32[]{:S(2)}, u32[]{:S(2)}) async-start(bf16[1,2,256,256]{3,1,0,2:T(2,128)(2,1)} %bitcast.124), calls=%async_computation.1 | async-start | bytes 524288 | tf_op jit(solution)/shard_map/all_to_all | solution.py:93
  46.2 2.0 %collective-permute-start.5 = (bf16[2,112,256]{2,1,0:T(8,128)(2,1)S(1)}, bf16[2,112,256]{2,1,0:T(8,128)(2,1)S(1)}, u32[]{:S(2)}, u32[]{:S(2)}) collective-permute-start(bf16[2,112,256]{2,1,0:T(8,128)(2,1)S(1)} %collective-permute-done.4), channel_id=1, source_target_pairs={{8,12},{9,13},{10,14},{11,15},{24,28},{25,29},{26,30},{27,31}} | collective-permute-start | bytes 344072 | tf_op jit(solution)/shard_map/ppermute | solution.py:50
  46.9 7.4 %collective-permute-start.2 = (bf16[2,112,256]{2,1,0:T(8,128)(2,1)S(1)}, bf16[2,112,256]{2,1,0:T(8,128)(2,1)S(1)}, u32[]{:S(2)}, u32[]{:S(2)}) collective-permute-start(bf16[2,112,256]{2,1,0:T(8,128)(2,1)S(1)} %collective-permute-done.1), channel_id=1, source_target_pairs={{4,0},{5,1},{6,2},{7,3},{20,16},{21,17},{22,18},{23,19}} | collective-permute-start | bytes 344072 | tf_op jit(solution)/shard_map/ppermute | solution.py:51
  55.8 9.4 %all-to-all-start = ((bf16[1,2,256,256]{3,1,0,2:T(2,128)(2,1)}), bf16[1,2,256,256]{3,1,0,2:T(2,128)(2,1)S(1)}, u32[]{:S(2)}, u32[]{:S(2)}) async-start(bf16[1,2,256,256]{3,1,0,2:T(2,128)(2,1)} %bitcast.113), calls=%async_computation | async-start | bytes 524288 | tf_op jit(solution)/shard_map/all_to_all | solution.py:93
where the time goes:
time: 70.3 us; the launch traced here: 69.7 us
  starting transfers between devices  33.8 us (48%)
  waiting for transfers between devices  22.8 us (32%)
  other arithmetic  5.77 us (8%)
  matrix products  3.87 us (6%)
  local copies, waits for them, and re-layouts  2.97 us (4%)
    ppermute x2, waiting for transfers between devices, relay_exchange(): down3 = lax.ppermute(down2, 'tile', [(1, 0)])  10.1 us
    ppermute x2, starting transfers between devices, relay_exchange(): up2 = lax.ppermute(jnp.where(t == 0, own[0], up1), 'tile', up)  9.53 us
    ppermute x2, starting transfers between devices, relay_exchange(): up1 = lax.ppermute(own[1], 'tile', up)  8.42 us
    all_to_all x2, starting transfers between devices, per_device(): lax.all_to_all(spectrum[None], 'freq', split_axis=2, concat_axis=0, tiled...  6.81 us
    all_to_all x2, waiting for transfers between devices, per_device(): lax.all_to_all(spectrum[None], 'freq', split_axis=2, concat_axis=0, tiled...  5.95 us
    ppermute x2, waiting for transfers between devices, relay_exchange(): down1 = lax.ppermute(own[0], 'tile', down)  4.4 us
    select_n x1, other arithmetic, per_device(): return jnp.where(inside, traces, jnp.float32(0.0))  4.26 us
    dot_general x2, matrix products, column_products(): lax.dot_general(v_local, x_local, (((3,), (1,)), ((), ())), preferred_ele...  2.94 us
  transfers between devices with their start and end apart: 14, of which 5 were waited for; matrix products, arithmetic and copies ran while one was open for 5% of the time, Pallas kernels for 0%

commit v1 on v0

--- a/solution.py
+++ b/solution.py
@@ -7,6 +7,30 @@
 NT = 32
 S_CHUNKS = 2
 first_bin = 2
+
+
+def split_up(x, dim, count):
+    lengths = x.shape
+    blocks = x.reshape(*lengths[:dim], count, lengths[dim] // count, *lengths[dim + 1 :])
+    return jnp.moveaxis(blocks, dim, 0)
+
+
+def laid_out(blocks, dim):
+    shape = list(blocks.shape[1:])
+    shape[dim] *= blocks.shape[0]
+    return jnp.moveaxis(blocks, 0, dim).reshape(shape)
+
+
+def exchange_directly(x, axis, split_dim, concat_dim):
+    size, index = (lax.axis_size(axis), lax.axis_index(axis))
+    parts = split_up(x, split_dim, size)
+    out = parts
+    for step in range(1, size):
+        target, source = ((index + step) % size, (index - step) % size)
+        sent = lax.dynamic_index_in_dim(parts, target, 0)
+        other = lax.ppermute(sent, axis, [(i, (i + step) % size) for i in range(size)])
+        out = lax.dynamic_update_slice_in_dim(out, other, source, axis=0)
+    return laid_out(out, concat_dim)
 
 
 def inverse_tables(count_freq, count_time):
@@ -89,9 +113,7 @@
                 spectrum = relay_exchange(own, u_local)
             else:
                 spectrum = gather_exchange(own, u_local, n_tile)
-            received_parts.append(
-                lax.all_to_all(spectrum[None], "freq", split_axis=2, concat_axis=0, tiled=True)
-            )
+            received_parts.append(exchange_directly(spectrum[None], "freq", 2, 0))
         received = jnp.concatenate(received_parts, axis=3) if chunks > 1 else received_parts[0]
         count_freq = received.shape[0]
         cosine_table, sine_table = inverse_tables(count_freq, NT)

time: 70.3 us -> 58 us (0.83)
  waiting for transfers between devices: 22.8 us -> 16.2 us
  starting transfers between devices: 33.8 us -> 29.8 us
  local copies, waits for them, and re-layouts: 2.97 us -> 1.3 us
    ppermute x2, waiting for transfers between devices: 10.1 us -> 2.9 us  [relay_exchange(): down3 = lax.ppermute(down2, 'tile', [(1, 0)])]
    all_to_all x2 -> x0, starting transfers between devices: 6.81 us -> none  [per_device(): lax.all_to_all(spectrum[None], 'freq', split_axis=2, concat_axis=0, tiled...]
    all_to_all x2 -> x0, waiting for transfers between devices: 5.95 us -> none  [per_device(): lax.all_to_all(spectrum[None], 'freq', split_axis=2, concat_axis=0, tiled...]
    ppermute x0 -> x6, waiting for transfers between devices: none -> 4.61 us  [exchange_directly(): lax.ppermute(sent, axis, [(i, (i + step) % size) for i in range(size)])]
    ppermute x0 -> x6, starting transfers between devices: none -> 3.4 us  [exchange_directly(): lax.ppermute(sent, axis, [(i, (i + step) % size) for i in range(size)])]
    ppermute x2, waiting for transfers between devices: 0.04 us -> 2.69 us  [relay_exchange(): down2 = lax.ppermute(jnp.where(t == 3, own[1], down1), 'tile', down)]
    unnamed x9 -> x7, local copies, waits for them, and re-layouts: 2.78 us -> 1.05 us
  transfers between devices with their start and end apart: 14 -> 18, of which waited for: 5 -> 8; matrix products, arithmetic and copies ran while one was open for 5% -> 3% of each run, Pallas kernels for 0% -> 0%
where the time goes in v1:
time: 58 us; the launch traced here: 57.5 us
  starting transfers between devices  29.8 us (51%)
  waiting for transfers between devices  16.2 us (28%)
  other arithmetic  5.76 us (10%)
  matrix products  3.85 us (7%)
  local copies, waits for them, and re-layouts  1.3 us (2%)
    ppermute x2, starting transfers between devices, relay_exchange(): up2 = lax.ppermute(jnp.where(t == 0, own[0], up1), 'tile', up)  8.89 us
    ppermute x2, starting transfers between devices, relay_exchange(): up1 = lax.ppermute(own[1], 'tile', up)  8.42 us
    ppermute x6, waiting for transfers between devices, exchange_directly(): lax.ppermute(sent, axis, [(i, (i + step) % size) for i in range(size)])  4.61 us
    select_n x1, other arithmetic, per_device(): return jnp.where(inside, traces, jnp.float32(0.0))  4.26 us
    ppermute x2, waiting for transfers between devices, relay_exchange(): down1 = lax.ppermute(own[0], 'tile', down)  4.05 us
    ppermute x6, starting transfers between devices, exchange_directly(): lax.ppermute(sent, axis, [(i, (i + step) % size) for i in range(size)])  3.4 us
    ppermute x2, waiting for transfers between devices, relay_exchange(): down3 = lax.ppermute(down2, 'tile', [(1, 0)])  2.9 us
    dot_general x2, matrix products, column_products(): lax.dot_general(v_local, x_local, (((3,), (1,)), ((), ())), preferred_ele...  2.88 us
  transfers between devices with their start and end apart: 18, of which 8 were waited for; matrix products, arithmetic and copies ran while one was open for 3% of the time, Pallas kernels for 0%

profile of v1, /device:TPU:0, one launch (start us, length us, event | category | flops | bytes accessed | tf_op | source)
XLA Modules:
  0.0 57.5 jit_solution(9493087892814764330)
XLA Ops:
  0.0 1.0 %copy-done = bf16[1,1,2,2,112,512]{5,4,3,2,1,0:T(8,128)(2,1)S(1)} copy-done((bf16[1,1,2,2,112,512]{5,4,3,2,1,0:T(8,128)(2,1)S(1)}, bf16[1,1,2,2,112,512]{5,4,3,2,1,0:T(8,128)(2,1)}, u32[]{:S(2)}) %copy-start) | copy-done | bytes 458776
  1.0 1.4 %fusion.66 = f32[2,2,112,2,256]{4,2,3,1,0:T(8,128)S(1)} fusion(bf16[2,512,512]{2,1,0:T(8,128)(2,1)} %bitcast.299, bf16[1,1,2,2,112,512]{5,4,3,2,1,0:T(8,128)(2,1)S(1)} %copy-done), kind=kOutput, calls=%fused_computation.111 | convolution fusion | flops 234881024 | bytes 1900544 | tf_op jit(solution)/shard_map/dot_general | solution.py:45
  2.5 1.4 %fusion.65 = f32[2,2,112,2,256]{4,2,0,3,1:T(8,128)S(1)} fusion(bf16[2,512,512]{2,1,0:T(8,128)(2,1)} %bitcast.300, bf16[1,1,2,2,112,512]{5,4,3,2,1,0:T(8,128)(2,1)S(1)} %copy-done), kind=kOutput, calls=%fused_computation.109 | convolution fusion | flops 234881024 | bytes 1900544 | tf_op jit(solution)/shard_map/dot_general | solution.py:45
  3.9 0.7 %iota_compare_fusion.2 = pred[2,112]{1,0:T(4,128)(4,1)S(1)} fusion(s32[2]{0:T(128)} %bitcast.349), kind=kLoop, calls=%fused_computation.187 | loop fusion | flops 224 | bytes 232 | tf_op jit(solution)/shard_map/lt | solution.py:51
  4.6 0.1 fusion.77
  4.7 0.1 fusion.74
  4.9 4.9 %collective-permute-start.3 = (bf16[2,112,256]{2,1,0:T(8,128)(2,1)S(1)}, bf16[2,112,256]{2,1,0:T(8,128)(2,1)S(1)}, u32[]{:S(2)}, u32[]{:S(2)}) collective-permute-start(bf16[2,112,256]{2,1,0:T(8,128)(2,1)S(1)} %fusion.90), channel_id=1, source_target_pairs={{0,4},{4,8},{8,12},{1,5},{5,9},{9,13},{2,6},{6,10},{10,14},{3,7},{... | collective-permute-start | bytes 344072 | tf_op jit(solution)/shard_map/ppermute | solution.py:70
  9.9 3.5 %collective-permute-start.12 = (bf16[2,112,256]{2,1,0:T(8,128)(2,1)S(1)}, bf16[2,112,256]{2,1,0:T(8,128)(2,1)S(1)}, u32[]{:S(2)}, u32[]{:S(2)}) collective-permute-start(bf16[2,112,256]{2,1,0:T(8,128)(2,1)S(1)} %fusion.86), channel_id=1, source_target_pairs={{0,4},{4,8},{8,12},{1,5},{5,9},{9,13},{2,6},{6,10},{10,14},{3,7},{... | collective-permute-start | bytes 344072 | tf_op jit(solution)/shard_map/ppermute | solution.py:70
  13.5 0.1 fusion.95
  13.8 1.9 %collective-permute-done.12 = bf16[2,112,256]{2,1,0:T(8,128)(2,1)S(1)} collective-permute-done((bf16[2,112,256]{2,1,0:T(8,128)(2,1)S(1)}, bf16[2,112,256]{2,1,0:T(8,128)(2,1)S(1)}, u32[]{:S(2)}, u32[]{:S(2)}) %collective-permute-start.12) | collective-permute-done | bytes 114720 | tf_op jit(solution)/shard_map/ppermute | solution.py:70
  15.7 4.3 %collective-permute-start.13 = (bf16[2,112,256]{2,1,0:T(8,128)(2,1)S(1)}, bf16[2,112,256]{2,1,0:T(8,128)(2,1)S(1)}, u32[]{:S(2)}, u32[]{:S(2)}) collective-permute-start(bf16[2,112,256]{2,1,0:T(8,128)(2,1)S(1)} %get-tuple-element.169), channel_id=1, source_target_pairs={{0,4},{4,8},{8,12},{1,5},{5,9},{9,13},{2,6},{6,10},{10,14},{3,7},{... | collective-permute-start | bytes 344072 | tf_op jit(solution)/shard_map/ppermute | solution.py:72
  20.1 1.3 %collective-permute-start.9 = (bf16[2,112,256]{2,1,0:T(8,128)(2,1)S(1)}, bf16[2,112,256]{2,1,0:T(8,128)(2,1)S(1)}, u32[]{:S(2)}, u32[]{:S(2)}) collective-permute-start(bf16[2,112,256]{2,1,0:T(8,128)(2,1)S(1)} %get-tuple-element.170), channel_id=1, source_target_pairs={{4,0},{8,4},{12,8},{5,1},{9,5},{13,9},{6,2},{10,6},{14,10},{7,3},{... | collective-permute-start | bytes 344072 | tf_op jit(solution)/shard_map/ppermute | solution.py:71
  21.4 0.0 collective-permute-done.3
  21.4 4.6 %collective-permute-start.4 = (bf16[2,112,256]{2,1,0:T(8,128)(2,1)S(1)}, bf16[2,112,256]{2,1,0:T(8,128)(2,1)S(1)}, u32[]{:S(2)}, u32[]{:S(2)}) collective-permute-start(bf16[2,112,256]{2,1,0:T(8,128)(2,1)S(1)} %get-tuple-element.167), channel_id=1, source_target_pairs={{0,4},{4,8},{8,12},{1,5},{5,9},{9,13},{2,6},{6,10},{10,14},{3,7},{... | collective-permute-start | bytes 344072 | tf_op jit(solution)/shard_map/ppermute | solution.py:72
  26.0 1.3 %collective-permute-start = (bf16[2,112,256]{2,1,0:T(8,128)(2,1)S(1)}, bf16[2,112,256]{2,1,0:T(8,128)(2,1)S(1)}, u32[]{:S(2)}, u32[]{:S(2)}) collective-permute-start(bf16[2,112,256]{2,1,0:T(8,128)(2,1)S(1)} %get-tuple-element.168), channel_id=1, source_target_pairs={{4,0},{8,4},{12,8},{5,1},{9,5},{13,9},{6,2},{10,6},{14,10},{7,3},{... | collective-permute-start | bytes 344072 | tf_op jit(solution)/shard_map/ppermute | solution.py:71
  27.3 0.0 collective-permute-done.9
  27.3 1.3 %collective-permute-start.10 = (bf16[2,112,256]{2,1,0:T(8,128)(2,1)S(1)}, bf16[2,112,256]{2,1,0:T(8,128)(2,1)S(1)}, u32[]{:S(2)}, u32[]{:S(2)}) collective-permute-start(bf16[2,112,256]{2,1,0:T(8,128)(2,1)S(1)} %broadcast_select_fusion.2), channel_id=1, source_target_pairs={{4,0},{8,4},{12,8},{5,1},{9,5},{13,9},{6,2},{10,6},{14,10},{7,3},{... | collective-permute-start | bytes 344072 | tf_op jit(solution)/shard_map/ppermute | solution.py:73
  28.6 4.1 %collective-permute-done = bf16[2,112,256]{2,1,0:T(8,128)(2,1)S(1)} collective-permute-done((bf16[2,112,256]{2,1,0:T(8,128)(2,1)S(1)}, bf16[2,112,256]{2,1,0:T(8,128)(2,1)S(1)}, u32[]{:S(2)}, u32[]{:S(2)}) %collective-permute-start) | collective-permute-done | bytes 114720 | tf_op jit(solution)/shard_map/ppermute | solution.py:71
  32.7 1.3 %collective-permute-start.1 = (bf16[2,112,256]{2,1,0:T(8,128)(2,1)S(1)}, bf16[2,112,256]{2,1,0:T(8,128)(2,1)S(1)}, u32[]{:S(2)}, u32[]{:S(2)}) collective-permute-start(bf16[2,112,256]{2,1,0:T(8,128)(2,1)S(1)} %broadcast_select_fusion.3), channel_id=1, source_target_pairs={{4,0},{8,4},{12,8},{5,1},{9,5},{13,9},{6,2},{10,6},{14,10},{7,3},{... | collective-permute-start | bytes 344072 | tf_op jit(solution)/shard_map/ppermute | solution.py:73
  34.0 0.0 collective-permute-done.13
  34.0 0.7 %collective-permute-start.14 = (bf16[2,112,256]{2,1,0:T(8,128)(2,1)S(1)}, bf16[2,112,256]{2,1,0:T(8,128)(2,1)S(1)}, u32[]{:S(2)}, u32[]{:S(2)}) collective-permute-start(bf16[2,112,256]{2,1,0:T(8,128)(2,1)S(1)} %collective-permute-done.13), channel_id=1, source_target_pairs={{8,12},{9,13},{10,14},{11,15},{24,28},{25,29},{26,30},{27,31}} | collective-permute-start | bytes 344072 | tf_op jit(solution)/shard_map/ppermute | solution.py:74
  34.7 0.0 collective-permute-done.4
  34.7 0.7 %collective-permute-start.5 = (bf16[2,112,256]{2,1,0:T(8,128)(2,1)S(1)}, bf16[2,112,256]{2,1,0:T(8,128)(2,1)S(1)}, u32[]{:S(2)}, u32[]{:S(2)}) collective-permute-start(bf16[2,112,256]{2,1,0:T(8,128)(2,1)S(1)} %collective-permute-done.4), channel_id=1, source_target_pairs={{8,12},{9,13},{10,14},{11,15},{24,28},{25,29},{26,30},{27,31}} | collective-permute-start | bytes 344072 | tf_op jit(solution)/shard_map/ppermute | solution.py:74
  35.4 0.3 collective-permute-done.10
  35.6 1.3 %collective-permute-start.11 = (bf16[2,112,256]{2,1,0:T(8,128)(2,1)S(1)}, bf16[2,112,256]{2,1,0:T(8,128)(2,1)S(1)}, u32[]{:S(2)}, u32[]{:S(2)}) collective-permute-start(bf16[2,112,256]{2,1,0:T(8,128)(2,1)S(1)} %collective-permute-done.10), channel_id=1, source_target_pairs={{4,0},{5,1},{6,2},{7,3},{20,16},{21,17},{22,18},{23,19}} | collective-permute-start | bytes 344072 | tf_op jit(solution)/shard_map/ppermute | solution.py:75
  36.9 2.4 %collective-permute-done.1 = bf16[2,112,256]{2,1,0:T(8,128)(2,1)S(1)} collective-permute-done((bf16[2,112,256]{2,1,0:T(8,128)(2,1)S(1)}, bf16[2,112,256]{2,1,0:T(8,128)(2,1)S(1)}, u32[]{:S(2)}, u32[]{:S(2)}) %collective-permute-start.1) | collective-permute-done | bytes 114720 | tf_op jit(solution)/shard_map/ppermute | solution.py:73
  39.4 1.3 %collective-permute-start.2 = (bf16[2,112,256]{2,1,0:T(8,128)(2,1)S(1)}, bf16[2,112,256]{2,1,0:T(8,128)(2,1)S(1)}, u32[]{:S(2)}, u32[]{:S(2)}) collective-permute-start(bf16[2,112,256]{2,1,0:T(8,128)(2,1)S(1)} %collective-permute-done.1), channel_id=1, source_target_pairs={{4,0},{5,1},{6,2},{7,3},{20,16},{21,17},{22,18},{23,19}} | collective-permute-start | bytes 344072 | tf_op jit(solution)/shard_map/ppermute | solution.py:75
  40.7 0.0 collective-permute-done.14
  40.7 0.0 collective-permute-done.5
  40.7 2.0 %collective-permute-done.11 = bf16[2,112,256]{2,1,0:T(8,128)(2,1)S(1)} collective-permute-done((bf16[2,112,256]{2,1,0:T(8,128)(2,1)S(1)}, bf16[2,112,256]{2,1,0:T(8,128)(2,1)S(1)}, u32[]{:S(2)}, u32[]{:S(2)}) %collective-permute-start.11) | collective-permute-done | bytes 114720 | tf_op jit(solution)/shard_map/ppermute | solution.py:75
  42.7 0.6 %conditional.7 = (bf16[1,2,4,64,256]{4,3,2,1,0:T(8,128)(2,1)S(1)}) conditional(s32[]{:T(128)} %clamp.4, (bf16[2,2,112,256]{3,2,1,0:T(8,128)(2,1)S(1)}, bf16[2,112,256]{2,1,0:T(8,128)(2,1)S(1)}, bf16[2,112,256]{2,1,0:T(8,128)(2,1)S(1)}, bf16[2,112,256]{2,1,0:T(8,128)(2,1)S(1)}, ...), branch_computations={%region_4.5_spmd, %region_5.6_spmd, %region_6.7_spmd, %region_7.8_... | conditional | flops 237109248 | bytes 4489224
  42.7 0.5 convolution_bitcast_fusion.4
  43.2 0.1 slice_subtract_fusion.4
  43.3 0.1 collective-permute-start.17
  43.4 1.6 %collective-permute-start.16 = (bf16[1,1,2,64,256]{4,3,2,1,0:T(8,128)(2,1)S(1)}, bf16[1,1,2,64,256]{4,3,2,1,0:T(8,128)(2,1)S(1)}, u32[]{:S(2)}, u32[]{:S(2)}) collective-permute-start(bf16[1,1,2,64,256]{4,3,2,1,0:T(8,128)(2,1)S(1)} %get-tuple-element.203), channel_id=1, source_target_pairs={{0,2},{1,3},{2,0},{3,1},{4,6},{5,7},{6,4},{7,5},{8,10},{9,11},{10,... | collective-permute-start | bytes 196616 | tf_op jit(solution)/shard_map/ppermute | solution.py:31
  45.0 0.2 collective-permute-start.15
  45.1 0.9 %collective-permute-done.2 = bf16[2,112,256]{2,1,0:T(8,128)(2,1)S(1)} collective-permute-done((bf16[2,112,256]{2,1,0:T(8,128)(2,1)S(1)}, bf16[2,112,256]{2,1,0:T(8,128)(2,1)S(1)}, u32[]{:S(2)}, u32[]{:S(2)}) %collective-permute-start.2) | collective-permute-done | bytes 114720 | tf_op jit(solution)/shard_map/ppermute | solution.py:75
  46.0 0.6 %conditional.6 = (bf16[1,2,4,64,256]{4,3,2,1,0:T(8,128)(2,1)S(1)}) conditional(s32[]{:T(128)} %clamp.4, (bf16[2,2,112,256]{3,2,0,1:T(8,128)(2,1)S(1)}, bf16[2,112,256]{2,1,0:T(8,128)(2,1)S(1)}, bf16[2,112,256]{2,1,0:T(8,128)(2,1)S(1)}, bf16[2,112,256]{2,1,0:T(8,128)(2,1)S(1)}, ...), branch_computations={%region_0.1_spmd, %region_1.2_spmd, %region_2.3_spmd, %region_3.4_... | conditional | flops 237109248 | bytes 4030472
  46.1 0.5 convolution_bitcast_fusion
  46.5 0.1 slice_subtract_fusion
  46.7 0.7 %collective-permute-start.8 = (bf16[1,1,2,64,256]{4,3,2,1,0:T(8,128)(2,1)S(1)}, bf16[1,1,2,64,256]{4,3,2,1,0:T(8,128)(2,1)S(1)}, u32[]{:S(2)}, u32[]{:S(2)}) collective-permute-start(bf16[1,1,2,64,256]{4,3,2,1,0:T(8,128)(2,1)S(1)} %get-tuple-element.199), channel_id=1, source_target_pairs={{0,3},{1,0},{2,1},{3,2},{4,7},{5,4},{6,5},{7,6},{8,11},{9,8},{10,9... | collective-permute-start | bytes 196616 | tf_op jit(solution)/shard_map/ppermute | solution.py:31
  47.4 0.9 %collective-permute-start.7 = (bf16[1,1,2,64,256]{4,3,2,1,0:T(8,128)(2,1)S(1)}, bf16[1,1,2,64,256]{4,3,2,1,0:T(8,128)(2,1)S(1)}, u32[]{:S(2)}, u32[]{:S(2)}) collective-permute-start(bf16[1,1,2,64,256]{4,3,2,1,0:T(8,128)(2,1)S(1)} %get-tuple-element.200), channel_id=1, source_target_pairs={{0,2},{1,3},{2,0},{3,1},{4,6},{5,7},{6,4},{7,5},{8,10},{9,11},{10,... | collective-permute-start | bytes 196616 | tf_op jit(solution)/shard_map/ppermute | solution.py:31
  48.3 0.9 %collective-permute-done.15 = bf16[1,1,2,64,256]{4,3,2,1,0:T(8,128)(2,1)S(1)} collective-permute-done((bf16[1,1,2,64,256]{4,3,2,1,0:T(8,128)(2,1)S(1)}, bf16[1,1,2,64,256]{4,3,2,1,0:T(8,128)(2,1)S(1)}, u32[]{:S(2)}, u32[]{:S(2)}) %collective-permute-start.15) | collective-permute-done | bytes 65568 | tf_op jit(solution)/shard_map/ppermute | solution.py:31
  49.2 0.0 collective-permute-start.6
  49.2 3.7 %collective-permute-done.6 = bf16[1,1,2,64,256]{4,3,2,1,0:T(8,128)(2,1)S(1)} collective-permute-done((bf16[1,1,2,64,256]{4,3,2,1,0:T(8,128)(2,1)S(1)}, bf16[1,1,2,64,256]{4,3,2,1,0:T(8,128)(2,1)S(1)}, u32[]{:S(2)}, u32[]{:S(2)}) %collective-permute-start.6) | collective-permute-done | bytes 65568 | tf_op jit(solution)/shard_map/ppermute | solution.py:31
  53.1 0.1 maximum_convert_fusion
  53.2 0.1 slice_bitcast_fusion.13
  53.3 4.3 %multiply_select_fusion = f32[64,32,512]{2,1,0:T(8,128)} fusion(f32[32]{0:T(128)S(1)} %get-tuple-element.210, f32[64,512]{1,0:T(8,128)S(1)} %get-tuple-element.188, f32[32]{0:T(128)S(1)} %get-tuple-element.211, f32[64,512]{1,0:T(8,128)S(1)} %get-tuple-element.189, f32[32]{0:T(128)S(1)} %get-tuple-element.212, f32[64,512]{1,0:T(8,128)S(1)} %get-tuple-element.190, ...), kind=kLoop, calls=%fused_computation.104 | loop fusion | flops 20971520 | bytes 5506048 | tf_op jit(solution)/shard_map/jit(_where)/select_n | solution.py:131
  (34 shorter events, 0.4 us)
Async XLA Ops:
  0.0 1.0 %copy-start = (bf16[1,1,2,2,112,512]{5,4,3,2,1,0:T(8,128)(2,1)S(1)}, bf16[1,1,2,2,112,512]{5,4,3,2,1,0:T(8,128)(2,1)}, u32[]{:S(2)}) copy-start(bf16[1,1,2,2,112,512]{5,4,3,2,1,0:T(8,128)(2,1)} %param.14) | copy-start | bytes 1376260
  0.0 13.6 %copy-start.2 = (s32[2,64,512]{2,1,0:T(8,128)S(1)}, s32[2,64,512]{2,1,0:T(8,128)}, u32[]{:S(2)}) copy-start(s32[2,64,512]{2,1,0:T(8,128)} %param.17) | copy-start | bytes 786436
  0.0 13.6 %copy-start.1 = (bf16[1,4,2,112,256]{4,3,2,1,0:T(8,128)(2,1)S(1)}, bf16[1,4,2,112,256]{4,3,2,1,0:T(8,128)(2,1)}, u32[]{:S(2)}) copy-start(bf16[1,4,2,112,256]{4,3,2,1,0:T(8,128)(2,1)} %param.15) | copy-start | bytes 1376260
  4.9 16.5 %collective-permute-start.3 = (bf16[2,112,256]{2,1,0:T(8,128)(2,1)S(1)}, bf16[2,112,256]{2,1,0:T(8,128)(2,1)S(1)}, u32[]{:S(2)}, u32[]{:S(2)}) collective-permute-start(bf16[2,112,256]{2,1,0:T(8,128)(2,1)S(1)} %fusion.90), channel_id=1, source_target_pairs={{0,4},{4,8},{8,12},{1,5},{5,9},{9,13},{2,6},{6,10},{10,14},{3,7},{... | collective-permute-start | bytes 344072 | tf_op jit(solution)/shard_map/ppermute | solution.py:70
  9.9 5.8 %collective-permute-start.12 = (bf16[2,112,256]{2,1,0:T(8,128)(2,1)S(1)}, bf16[2,112,256]{2,1,0:T(8,128)(2,1)S(1)}, u32[]{:S(2)}, u32[]{:S(2)}) collective-permute-start(bf16[2,112,256]{2,1,0:T(8,128)(2,1)S(1)} %fusion.86), channel_id=1, source_target_pairs={{0,4},{4,8},{8,12},{1,5},{5,9},{9,13},{2,6},{6,10},{10,14},{3,7},{... | collective-permute-start | bytes 344072 | tf_op jit(solution)/shard_map/ppermute | solution.py:70
  15.7 18.2 %collective-permute-start.13 = (bf16[2,112,256]{2,1,0:T(8,128)(2,1)S(1)}, bf16[2,112,256]{2,1,0:T(8,128)(2,1)S(1)}, u32[]{:S(2)}, u32[]{:S(2)}) collective-permute-start(bf16[2,112,256]{2,1,0:T(8,128)(2,1)S(1)} %get-tuple-element.169), channel_id=1, source_target_pairs={{0,4},{4,8},{8,12},{1,5},{5,9},{9,13},{2,6},{6,10},{10,14},{3,7},{... | collective-permute-start | bytes 344072 | tf_op jit(solution)/shard_map/ppermute | solution.py:72
  20.1 7.2 %collective-permute-start.9 = (bf16[2,112,256]{2,1,0:T(8,128)(2,1)S(1)}, bf16[2,112,256]{2,1,0:T(8,128)(2,1)S(1)}, u32[]{:S(2)}, u32[]{:S(2)}) collective-permute-start(bf16[2,112,256]{2,1,0:T(8,128)(2,1)S(1)} %get-tuple-element.170), channel_id=1, source_target_pairs={{4,0},{8,4},{12,8},{5,1},{9,5},{13,9},{6,2},{10,6},{14,10},{7,3},{... | collective-permute-start | bytes 344072 | tf_op jit(solution)/shard_map/ppermute | solution.py:71
  21.4 13.3 %collective-permute-start.4 = (bf16[2,112,256]{2,1,0:T(8,128)(2,1)S(1)}, bf16[2,112,256]{2,1,0:T(8,128)(2,1)S(1)}, u32[]{:S(2)}, u32[]{:S(2)}) collective-permute-start(bf16[2,112,256]{2,1,0:T(8,128)(2,1)S(1)} %get-tuple-element.167), channel_id=1, source_target_pairs={{0,4},{4,8},{8,12},{1,5},{5,9},{9,13},{2,6},{6,10},{10,14},{3,7},{... | collective-permute-start | bytes 344072 | tf_op jit(solution)/shard_map/ppermute | solution.py:72
  26.0 6.7 %collective-permute-start = (bf16[2,112,256]{2,1,0:T(8,128)(2,1)S(1)}, bf16[2,112,256]{2,1,0:T(8,128)(2,1)S(1)}, u32[]{:S(2)}, u32[]{:S(2)}) collective-permute-start(bf16[2,112,256]{2,1,0:T(8,128)(2,1)S(1)} %get-tuple-element.168), channel_id=1, source_target_pairs={{4,0},{8,4},{12,8},{5,1},{9,5},{13,9},{6,2},{10,6},{14,10},{7,3},{... | collective-permute-start | bytes 344072 | tf_op jit(solution)/shard_map/ppermute | solution.py:71
  27.3 8.3 %collective-permute-start.10 = (bf16[2,112,256]{2,1,0:T(8,128)(2,1)S(1)}, bf16[2,112,256]{2,1,0:T(8,128)(2,1)S(1)}, u32[]{:S(2)}, u32[]{:S(2)}) collective-permute-start(bf16[2,112,256]{2,1,0:T(8,128)(2,1)S(1)} %broadcast_select_fusion.2), channel_id=1, source_target_pairs={{4,0},{8,4},{12,8},{5,1},{9,5},{13,9},{6,2},{10,6},{14,10},{7,3},{... | collective-permute-start | bytes 344072 | tf_op jit(solution)/shard_map/ppermute | solution.py:73
  32.7 6.7 %collective-permute-start.1 = (bf16[2,112,256]{2,1,0:T(8,128)(2,1)S(1)}, bf16[2,112,256]{2,1,0:T(8,128)(2,1)S(1)}, u32[]{:S(2)}, u32[]{:S(2)}) collective-permute-start(bf16[2,112,256]{2,1,0:T(8,128)(2,1)S(1)} %broadcast_select_fusion.3), channel_id=1, source_target_pairs={{4,0},{8,4},{12,8},{5,1},{9,5},{13,9},{6,2},{10,6},{14,10},{7,3},{... | collective-permute-start | bytes 344072 | tf_op jit(solution)/shard_map/ppermute | solution.py:73
  34.0 6.7 %collective-permute-start.14 = (bf16[2,112,256]{2,1,0:T(8,128)(2,1)S(1)}, bf16[2,112,256]{2,1,0:T(8,128)(2,1)S(1)}, u32[]{:S(2)}, u32[]{:S(2)}) collective-permute-start(bf16[2,112,256]{2,1,0:T(8,128)(2,1)S(1)} %collective-permute-done.13), channel_id=1, source_target_pairs={{8,12},{9,13},{10,14},{11,15},{24,28},{25,29},{26,30},{27,31}} | collective-permute-start | bytes 344072 | tf_op jit(solution)/shard_map/ppermute | solution.py:74
  34.7 6.0 %collective-permute-start.5 = (bf16[2,112,256]{2,1,0:T(8,128)(2,1)S(1)}, bf16[2,112,256]{2,1,0:T(8,128)(2,1)S(1)}, u32[]{:S(2)}, u32[]{:S(2)}) collective-permute-start(bf16[2,112,256]{2,1,0:T(8,128)(2,1)S(1)} %collective-permute-done.4), channel_id=1, source_target_pairs={{8,12},{9,13},{10,14},{11,15},{24,28},{25,29},{26,30},{27,31}} | collective-permute-start | bytes 344072 | tf_op jit(solution)/shard_map/ppermute | solution.py:74
  35.6 7.0 %collective-permute-start.11 = (bf16[2,112,256]{2,1,0:T(8,128)(2,1)S(1)}, bf16[2,112,256]{2,1,0:T(8,128)(2,1)S(1)}, u32[]{:S(2)}, u32[]{:S(2)}) collective-permute-start(bf16[2,112,256]{2,1,0:T(8,128)(2,1)S(1)} %collective-permute-done.10), channel_id=1, source_target_pairs={{4,0},{5,1},{6,2},{7,3},{20,16},{21,17},{22,18},{23,19}} | collective-permute-start | bytes 344072 | tf_op jit(solution)/shard_map/ppermute | solution.py:75
  39.4 6.7 %collective-permute-start.2 = (bf16[2,112,256]{2,1,0:T(8,128)(2,1)S(1)}, bf16[2,112,256]{2,1,0:T(8,128)(2,1)S(1)}, u32[]{:S(2)}, u32[]{:S(2)}) collective-permute-start(bf16[2,112,256]{2,1,0:T(8,128)(2,1)S(1)} %collective-permute-done.1), channel_id=1, source_target_pairs={{4,0},{5,1},{6,2},{7,3},{20,16},{21,17},{22,18},{23,19}} | collective-permute-start | bytes 344072 | tf_op jit(solution)/shard_map/ppermute | solution.py:75
  43.3 9.7 %collective-permute-start.17 = (bf16[1,1,2,64,256]{4,3,2,1,0:T(8,128)(2,1)S(1)}, bf16[1,1,2,64,256]{4,3,2,1,0:T(8,128)(2,1)S(1)}, u32[]{:S(2)}, u32[]{:S(2)}) collective-permute-start(bf16[1,1,2,64,256]{4,3,2,1,0:T(8,128)(2,1)S(1)} %get-tuple-element.202), channel_id=1, source_target_pairs={{0,3},{1,0},{2,1},{3,2},{4,7},{5,4},{6,5},{7,6},{8,11},{9,8},{10,9... | collective-permute-start | bytes 196616 | tf_op jit(solution)/shard_map/ppermute | solution.py:31
  43.4 9.5 %collective-permute-start.16 = (bf16[1,1,2,64,256]{4,3,2,1,0:T(8,128)(2,1)S(1)}, bf16[1,1,2,64,256]{4,3,2,1,0:T(8,128)(2,1)S(1)}, u32[]{:S(2)}, u32[]{:S(2)}) collective-permute-start(bf16[1,1,2,64,256]{4,3,2,1,0:T(8,128)(2,1)S(1)} %get-tuple-element.203), channel_id=1, source_target_pairs={{0,2},{1,3},{2,0},{3,1},{4,6},{5,7},{6,4},{7,5},{8,10},{9,11},{10,... | collective-permute-start | bytes 196616 | tf_op jit(solution)/shard_map/ppermute | solution.py:31
  45.0 4.3 %collective-permute-start.15 = (bf16[1,1,2,64,256]{4,3,2,1,0:T(8,128)(2,1)S(1)}, bf16[1,1,2,64,256]{4,3,2,1,0:T(8,128)(2,1)S(1)}, u32[]{:S(2)}, u32[]{:S(2)}) collective-permute-start(bf16[1,1,2,64,256]{4,3,2,1,0:T(8,128)(2,1)S(1)} %get-tuple-element.204), channel_id=1, source_target_pairs={{0,1},{1,2},{2,3},{3,0},{4,5},{5,6},{6,7},{7,4},{8,9},{9,10},{10,1... | collective-permute-start | bytes 196616 | tf_op jit(solution)/shard_map/ppermute | solution.py:31
  46.7 6.3 %collective-permute-start.8 = (bf16[1,1,2,64,256]{4,3,2,1,0:T(8,128)(2,1)S(1)}, bf16[1,1,2,64,256]{4,3,2,1,0:T(8,128)(2,1)S(1)}, u32[]{:S(2)}, u32[]{:S(2)}) collective-permute-start(bf16[1,1,2,64,256]{4,3,2,1,0:T(8,128)(2,1)S(1)} %get-tuple-element.199), channel_id=1, source_target_pairs={{0,3},{1,0},{2,1},{3,2},{4,7},{5,4},{6,5},{7,6},{8,11},{9,8},{10,9... | collective-permute-start | bytes 196616 | tf_op jit(solution)/shard_map/ppermute | solution.py:31
  47.4 5.6 %collective-permute-start.7 = (bf16[1,1,2,64,256]{4,3,2,1,0:T(8,128)(2,1)S(1)}, bf16[1,1,2,64,256]{4,3,2,1,0:T(8,128)(2,1)S(1)}, u32[]{:S(2)}, u32[]{:S(2)}) collective-permute-start(bf16[1,1,2,64,256]{4,3,2,1,0:T(8,128)(2,1)S(1)} %get-tuple-element.200), channel_id=1, source_target_pairs={{0,2},{1,3},{2,0},{3,1},{4,6},{5,7},{6,4},{7,5},{8,10},{9,11},{10,... | collective-permute-start | bytes 196616 | tf_op jit(solution)/shard_map/ppermute | solution.py:31
  49.2 3.7 %collective-permute-start.6 = (bf16[1,1,2,64,256]{4,3,2,1,0:T(8,128)(2,1)S(1)}, bf16[1,1,2,64,256]{4,3,2,1,0:T(8,128)(2,1)S(1)}, u32[]{:S(2)}, u32[]{:S(2)}) collective-permute-start(bf16[1,1,2,64,256]{4,3,2,1,0:T(8,128)(2,1)S(1)} %get-tuple-element.201), channel_id=1, source_target_pairs={{0,1},{1,2},{2,3},{3,0},{4,5},{5,6},{6,7},{7,4},{8,9},{9,10},{10,1... | collective-permute-start | bytes 196616 | tf_op jit(solution)/shard_map/ppermute | solution.py:31
